TPU v7x, 512 devices: a whole 4x8x8 slice. The times are simulated.
512 devices in a mesh: tm: 32 (over y, x), rows: 16 (over z, core).
Axes of the slice: x: 4, y: 8, z: 8, core: 2. Of those that a mesh axis runs over, the one named last changes fastest.
Arguments:
- features: bfloat16 [64, 16, 40, 384], P('tm', 'rows'), may hold values from -6 to 6
- gain_one: float32 [384], replicated, may hold values from 0.1 to 1.9
- weight_one: bfloat16 [384, 3, 3, 3, 384], P('rows'), may hold values from -0.0625 to 0.0625
- bias_one: float32 [384], replicated, may hold values from -3 to 3
- gain_two: float32 [384], replicated, may hold values from 0.1 to 1.9
- weight_two: bfloat16 [384, 3, 3, 3, 384], P('rows'), may hold values from -0.0625 to 0.0625
- bias_two: float32 [384], replicated, may hold values from -3 to 3
Outputs:
- block_out: bfloat16 [64, 16, 40, 384], P('tm', 'rows')
All inputs are finite; a program needn't handle non-finite values.
Results may differ from a plain program's by a relative error of at most 0.0049.
Values may be sent and summed in bfloat16 or wider, within the bound.
No kernel may reach another device: no remote copies, remote signals or barrier semaphores. Data moves between devices by JAX's collectives and lax.ppermute only.
A program may use at most 64 MiB of HBM per device.

v0:
```python
import jax
import jax.numpy as jnp
from jax import lax
from jax.sharding import PartitionSpec as P


def passed_along(x, axis, by):
    peers = lax.axis_size(axis)
    pairs = [(i, i + by) for i in range(peers) if 0 <= i + by < peers]
    return lax.ppermute(x, axis, pairs)


def norm_silu(values, norm_gain):
    values = values.astype(jnp.float32)
    mean_square = jnp.mean(values * values, axis=-1, keepdims=True)
    scaled = values * lax.rsqrt(mean_square + 1e-06) * norm_gain
    return jax.nn.silu(scaled).astype(jnp.bfloat16)


def causal_conv(extended, kernel, bias_part):
    frames = extended.shape[0] - 2
    height = extended.shape[1]
    columns = extended.shape[2]
    channels = extended.shape[3]
    part_width = kernel.shape[0]
    folded = 9 * part_width
    padded_width = (folded + 127) // 128 * 128
    padded = jnp.pad(extended, ((0, 0), (1, 1), (1, 1), (0, 0)))
    summed = jnp.zeros((frames, height, columns, part_width), jnp.float32)
    for tap_time in range(3):
        slab = padded[tap_time : tap_time + frames]
        taps = jnp.transpose(kernel[:, tap_time], (1, 2, 0, 3)).reshape(folded, channels)
        taps = jnp.pad(taps, ((0, padded_width - folded), (0, 0)))
        product = lax.dot_general(
            slab.reshape(-1, channels),
            taps,
            (((1,), (1,)), ((), ())),
            preferred_element_type=jnp.float32,
        )
        product = product[:, :folded].reshape(frames, height + 2, columns + 2, 3, 3, part_width)
        for tap_row in range(3):
            for tap_col in range(3):
                summed = (
                    summed
                    + product[
                        :, tap_row : tap_row + height, tap_col : tap_col + columns, tap_row, tap_col
                    ]
                )
    return summed + bias_part


def shards(features, gain_one, weight_one, bias_one, gain_two, weight_two, bias_two):
    part_width = weight_one.shape[0]
    offset = lax.axis_index("rows") * part_width
    bias_first = lax.dynamic_slice_in_dim(bias_one, offset, part_width, 0)
    bias_second = lax.dynamic_slice_in_dim(bias_two, offset, part_width, 0)
    normed_one = norm_silu(features, gain_one)
    prior_one = passed_along(normed_one, "tm", 1)
    extended_one = jnp.concatenate([prior_one, normed_one], 0)
    full_one = lax.all_gather(extended_one, "rows", axis=1, tiled=True)
    conv_one = causal_conv(full_one, weight_one, bias_first).astype(jnp.bfloat16)
    own_rows = lax.all_to_all(conv_one, "rows", split_axis=1, concat_axis=3, tiled=True)
    normed_two = norm_silu(own_rows, gain_two)
    prior_two = passed_along(normed_two, "tm", 1)
    extended_two = jnp.concatenate([prior_two, normed_two], 0)
    full_two = lax.all_gather(extended_two, "rows", axis=1, tiled=True)
    conv_two = causal_conv(full_two, weight_two, bias_second)
    returned = lax.all_to_all(conv_two, "rows", split_axis=1, concat_axis=3, tiled=True)
    return (features.astype(jnp.float32) + returned).astype(jnp.bfloat16)


def solution(mesh):
    in_specs = (
        P("tm", "rows", None, None),
        P(),
        P("rows", None, None, None, None),
        P(),
        P(),
        P("rows", None, None, None, None),
        P(),
    )
    out_specs = P("tm", "rows", None, None)
    return jax.shard_map(shards, mesh=mesh, in_specs=in_specs, out_specs=out_specs, check_vma=False)
```

profile of v0, /device:TPU:1, one launch (start us, length us, event | category | flops | bytes accessed | tf_op | source)
XLA Modules:
  0.0 217.8 jit_solution(14636832090744077345)
XLA Ops:
  6.5 0.9 fusion.25
  7.5 0.9 fusion.32
  8.4 3.9 %collective-permute-start = (bf16[2,1,40,384]{3,2,1,0:T(8,128)(2,1)S(1)}, bf16[2,1,40,384]{3,2,1,0:T(8,128)(2,1)S(1)}, u32[]{:S(2)}, u32[]{:S(2)}) collective-permute-start(bf16[2,1,40,384]{3,2,1,0:T(8,128)(2,1)S(1)} %fusion.32), channel_id=1, source_target_pairs={{0,16},{16,32},{32,48},{48,64},{64,80},{80,96},{96,112},{112,128},... | collective-permute-start | bytes 184328 | tf_op jit(solution)/shard_map/ppermute | solution.py:10
  12.4 1.3 collective-permute-done
  15.2 1.1 fusion.35
  16.3 48.9 %all-gather.3.cloned.1.call-done = bf16[4,16,40,384]{3,2,0,1:T(8,128)(2,1)} async-done(((bf16[4,1,40,384]{3,2,0,1:T(8,128)(2,1)}), bf16[4,16,40,384]{3,2,0,1:T(8,128)(2,1)}) %all-gather.3.cloned.1.call-update) | async-done | bytes 1966096 | tf_op jit(solution)/shard_map/all_gather | solution.py:60
  65.2 4.8 %pad_slice_fusion.5 = (bf16[2,18,42,384]{3,2,0,1:T(8,128)(2,1)S(1)}, bf16[2,18,42,384]{3,2,0,1:T(8,128)(2,1)}, bf16[2,18,42,384]{3,2,0,1:T(8,128)(2,1)S(1)}) fusion(bf16[4,16,40,384]{3,2,0,1:T(8,128)(2,1)} %all-gather.3.cloned.1.call-done), kind=kLoop, calls=%fused_computation.5 | loop fusion | bytes 5449728 | tf_op jit(solution)/shard_map/slice | solution.py:31
  70.2 1.3 reshape.154
  71.5 1.9 fusion.38
  73.4 4.3 %reshape.156 = f32[2,18,42,3,3,24]{2,1,0,5,4,3:T(8,128)} reshape(f32[1512,216]{0,1:T(8,128)S(1)} %fusion.38) | data formatting | bytes 2612736 | tf_op jit(solution)/shard_map/reshape | solution.py:40
  77.7 1.5 copy.58
  79.2 1.4 reshape.151
  80.5 1.9 fusion.37
  82.4 4.4 %reshape.153 = f32[2,18,42,3,3,24]{2,1,0,5,4,3:T(8,128)} reshape(f32[1512,216]{0,1:T(8,128)S(1)} %fusion.37) | data formatting | bytes 2612736 | tf_op jit(solution)/shard_map/reshape | solution.py:40
  87.9 4.3 %reshape.150 = f32[2,18,42,3,3,24]{2,1,0,5,4,3:T(8,128)} reshape(f32[1512,216]{0,1:T(8,128)S(1)} %fusion.36) | data formatting | bytes 2612736 | tf_op jit(solution)/shard_map/reshape | solution.py:40
  92.2 7.0 %fusion.14 = bf16[2,16,40,24]{2,1,0,3:T(8,128)(2,1)S(1)} fusion(f32[2,18,42,3,3,24]{2,1,0,5,4,3:T(8,128)} %reshape.156, f32[2,18,42,3,3,24]{2,1,0,5,4,3:T(8,128)} %reshape.153, f32[2,18,42,3,3,24]{2,1,0,5,4,3:T(8,128)} %reshape.150, f32[24]{0:T(128)S(1)} %dynamic_slice.6), kind=kLoop, calls=%fused_computation.47 | loop fusion | flops 860160 | bytes 3379296 | tf_op jit(solution)/shard_map/convert_element_type | solution.py:61
  99.6 12.0 %all_to_all.27 = bf16[16,2,960]{2,1,0:T(2,128)(2,1)S(1)} all-to-all(bf16[16,2,960]{2,1,0:T(2,128)(2,1)S(1)} %reshape.192), channel_id=1, replica_groups=mesh['tm'=32,'rows'=16] {'rows'}, dimensions={0} | all-to-all | bytes 122880 | tf_op jit(solution)/shard_map/all_to_all | solution.py:62
  112.7 3.3 %collective-permute-start.1 = (bf16[2,1,40,384]{3,2,1,0:T(8,128)(2,1)S(1)}, bf16[2,1,40,384]{3,2,1,0:T(8,128)(2,1)S(1)}, u32[]{:S(2)}, u32[]{:S(2)}) collective-permute-start(bf16[2,1,40,384]{3,2,1,0:T(8,128)(2,1)S(1)} %multiply_convert_fusion), channel_id=1, source_target_pairs={{0,16},{16,32},{32,48},{48,64},{64,80},{80,96},{96,112},{112,128},... | collective-permute-start | bytes 184328 | tf_op jit(solution)/shard_map/ppermute | solution.py:10
  116.0 1.1 collective-permute-done.1
  118.6 41.3 %all-gather.5.cloned.1.call-done = bf16[4,16,40,384]{3,2,0,1:T(8,128)(2,1)} async-done(((bf16[4,1,40,384]{3,2,0,1:T(8,128)(2,1)}), bf16[4,16,40,384]{3,2,0,1:T(8,128)(2,1)}) %all-gather.5.cloned.1.call-update) | async-done | bytes 1966096 | tf_op jit(solution)/shard_map/all_gather | solution.py:66
  159.9 4.8 %pad_slice_fusion.2 = (bf16[2,18,42,384]{3,2,0,1:T(8,128)(2,1)S(1)}, bf16[2,18,42,384]{3,2,0,1:T(8,128)(2,1)}, bf16[2,18,42,384]{3,2,0,1:T(8,128)(2,1)S(1)}) fusion(bf16[4,16,40,384]{3,2,0,1:T(8,128)(2,1)} %all-gather.5.cloned.1.call-done), kind=kLoop, calls=%fused_computation.2 | loop fusion | bytes 5449728 | tf_op jit(solution)/shard_map/slice | solution.py:31
  164.8 1.3 reshape.163
  166.1 1.9 fusion.41
  168.0 4.3 %reshape.165 = f32[2,18,42,3,3,24]{2,1,0,5,4,3:T(8,128)} reshape(f32[1512,216]{0,1:T(8,128)S(1)} %fusion.41) | data formatting | bytes 2612736 | tf_op jit(solution)/shard_map/reshape | solution.py:40
  172.4 1.5 copy.65
  173.8 1.4 reshape.160
  175.2 1.9 fusion.40
  177.1 4.4 %reshape.162 = f32[2,18,42,3,3,24]{2,1,0,5,4,3:T(8,128)} reshape(f32[1512,216]{0,1:T(8,128)S(1)} %fusion.40) | data formatting | bytes 2612736 | tf_op jit(solution)/shard_map/reshape | solution.py:40
  182.5 4.3 %reshape.159 = f32[2,18,42,3,3,24]{2,1,0,5,4,3:T(8,128)} reshape(f32[1512,216]{0,1:T(8,128)S(1)} %fusion.39) | data formatting | bytes 2612736 | tf_op jit(solution)/shard_map/reshape | solution.py:40
  186.8 7.0 %fusion.1 = f32[2,16,40,24]{2,1,0,3:T(8,128)S(1)} fusion(f32[2,18,42,3,3,24]{2,1,0,5,4,3:T(8,128)} %reshape.165, f32[2,18,42,3,3,24]{2,1,0,5,4,3:T(8,128)} %reshape.162, f32[2,18,42,3,3,24]{2,1,0,5,4,3:T(8,128)} %reshape.159, f32[24]{0:T(128)S(1)} %dynamic_slice.7), kind=kLoop, calls=%fused_computation.8 | loop fusion | flops 829440 | bytes 3440736 | tf_op jit(solution)/shard_map/add | solution.py:49
  194.8 13.2 %all_to_all.28 = f32[16,1,1920]{2,1,0:T(1,128)S(1)} all-to-all(f32[16,1,1920]{2,1,0:T(1,128)S(1)} %reshape.194), channel_id=1, replica_groups=mesh['tm'=32,'rows'=16] {'rows'}, dimensions={0} | all-to-all | bytes 245760 | tf_op jit(solution)/shard_map/all_to_all | solution.py:68
  208.5 0.9 reduce.5
  (38 shorter events, 9.8 us)
Async XLA Ops:
  6.5 58.7 %all-gather.3.cloned.1.call-start = ((), (), s32[]{:S(2)}) async-start(), calls=%async_computation.2 | async-start | bytes 2088960 | tf_op jit(solution)/shard_map/all_gather | solution.py:60
  8.4 5.2 %collective-permute-start = (bf16[2,1,40,384]{3,2,1,0:T(8,128)(2,1)S(1)}, bf16[2,1,40,384]{3,2,1,0:T(8,128)(2,1)S(1)}, u32[]{:S(2)}, u32[]{:S(2)}) collective-permute-start(bf16[2,1,40,384]{3,2,1,0:T(8,128)(2,1)S(1)} %fusion.32), channel_id=1, source_target_pairs={{0,16},{16,32},{32,48},{48,64},{64,80},{80,96},{96,112},{112,128},... | collective-permute-start | bytes 184328 | tf_op jit(solution)/shard_map/ppermute | solution.py:10
  14.3 145.5 %all-gather.5.cloned.1.call-start = ((), (), s32[]{:S(2)}) async-start(), calls=%async_computation.3 | async-start | bytes 2088960 | tf_op jit(solution)/shard_map/all_gather | solution.py:66
  99.2 13.4 %copy-start.2 = (f32[384]{0:T(512)S(1)}, f32[384]{0:T(512)}, u32[]{:S(2)}) copy-start(f32[384]{0:T(512)} %param.11) | copy-start | bytes 4612
  99.3 19.2 %copy-start.1 = (bf16[24,3,3,3,384]{4,0,3,2,1:T(8,128)(2,1)S(1)}, bf16[24,3,3,3,384]{4,0,3,2,1:T(8,128)(2,1)}, u32[]{:S(2)}) copy-start(bf16[24,3,3,3,384]{4,0,3,2,1:T(8,128)(2,1)} %param.12) | copy-start | bytes 1492996
  112.7 4.4 %collective-permute-start.1 = (bf16[2,1,40,384]{3,2,1,0:T(8,128)(2,1)S(1)}, bf16[2,1,40,384]{3,2,1,0:T(8,128)(2,1)S(1)}, u32[]{:S(2)}, u32[]{:S(2)}) collective-permute-start(bf16[2,1,40,384]{3,2,1,0:T(8,128)(2,1)S(1)} %multiply_convert_fusion), channel_id=1, source_target_pairs={{0,16},{16,32},{32,48},{48,64},{64,80},{80,96},{96,112},{112,128},... | collective-permute-start | bytes 184328 | tf_op jit(solution)/shard_map/ppermute | solution.py:10
  193.8 16.5 %copy-start = (bf16[2,1,40,384]{3,2,1,0:T(8,128)(2,1)S(1)}, bf16[2,1,40,384]{3,2,1,0:T(8,128)(2,1)}, u32[]{:S(2)}) copy-start(bf16[2,1,40,384]{3,2,1,0:T(8,128)(2,1)} %param.7) | copy-start | bytes 184324
Sparse Core Ops, SparseCore 0:
  14.5 50.7 all-gather.2
  117.9 41.9 all-gather.4
where the time goes:
time: 218 us
  waiting for transfers between devices  92.6 us (42%)
  local copies, waits for them, and re-layouts  50.8 us (23%)
  blocking collectives  25.2 us (12%)
  other arithmetic  19.4 us (9%)
  between operations  13.6 us (6%)
  matrix products  8.8 us (4%)
  starting transfers between devices  7.28 us (3%)
    all_gather x1, waiting for transfers between devices, shards(): full_one = lax.all_gather(extended_one, 'rows', axis=1, tiled=True)  48.9 us
    all_gather x1, waiting for transfers between devices, shards(): full_two = lax.all_gather(extended_two, 'rows', axis=1, tiled=True)  41.3 us
    reshape x6, local copies, waits for them, and re-layouts, causal_conv(): product[:, :folded]  25.9 us
    all_to_all x1, blocking collectives, shards(): lax.all_to_all(conv_two, 'rows', split_axis=1, concat_axis=3, tiled=True)  13.2 us
    slice x8, local copies, waits for them, and re-layouts, causal_conv(): slab = padded[tap_time:tap_time + frames]  13.1 us
    all_to_all x1, blocking collectives, shards(): lax.all_to_all(conv_one, 'rows', split_axis=1, concat_axis=3, tiled=True)  12 us
    dot_general x6, matrix products, causal_conv(): lax.dot_general(slab.reshape(-1, channels), taps, (((1,), (1,)), ((), ())...  8.8 us
    ppermute x2, starting transfers between devices, passed_along(): return lax.ppermute(x, axis, pairs)  7.24 us
  transfers between devices with their start and end apart: 4, of which 4 were waited for; matrix products, arithmetic and copies ran while one was open for 1% of the time, Pallas kernels for 0%

commit v1 on v0

--- a/solution.py
+++ b/solution.py
@@ -63,7 +63,9 @@
     normed_two = norm_silu(own_rows, gain_two)
     prior_two = passed_along(normed_two, "tm", 1)
     extended_two = jnp.concatenate([prior_two, normed_two], 0)
-    full_two = lax.all_gather(extended_two, "rows", axis=1, tiled=True)
+    full_two = jnp.concatenate(
+        lax.all_to_all(jnp.stack([extended_two] * lax.axis_size("rows")), "rows", 0, 0), axis=1
+    )
     conv_two = causal_conv(full_two, weight_two, bias_second)
     returned = lax.all_to_all(conv_two, "rows", split_axis=1, concat_axis=3, tiled=True)
     return (features.astype(jnp.float32) + returned).astype(jnp.bfloat16)

time: 218 us -> 229 us (1.050); the launches traced: 218 us -> 225 us
  starting transfers between devices: 7.28 us -> 11.7 us
  waiting for transfers between devices: 92.6 us -> 96.4 us
    all_to_all x0 -> x1, waiting for transfers between devices: none -> 44.8 us  [shards(): lax.all_to_all(jnp.stack([extended_two] * lax.axis_size('rows')), 'rows',...]
    all_gather x1 -> x0, waiting for transfers between devices: 41.3 us -> none  [shards(): full_two = lax.all_gather(extended_two, 'rows', axis=1, tiled=True)]
    all_to_all x0 -> x1, starting transfers between devices: none -> 4.65 us  [shards(): lax.all_to_all(jnp.stack([extended_two] * lax.axis_size('rows')), 'rows',...]
    slice x8, local copies, waits for them, and re-layouts: 13.1 us -> 10.6 us  [causal_conv(): slab = padded[tap_time:tap_time + frames]]
  transfers between devices with their start and end apart: 4 -> 4, of which waited for: 4 -> 4; matrix products, arithmetic and copies ran while one was open for 1% -> 2% of each run, Pallas kernels for 0% -> 0%
where the time goes in v1:
time: 229 us; the launch traced here: 225 us
  waiting for transfers between devices  96.4 us (42%)
  local copies, waits for them, and re-layouts  50.5 us (22%)
  blocking collectives  25.6 us (11%)
  other arithmetic  18.8 us (8%)
  between operations  13.6 us (6%)
  starting transfers between devices  11.7 us (5%)
  matrix products  8.78 us (4%)
    all_gather x1, waiting for transfers between devices, shards(): full_one = lax.all_gather(extended_one, 'rows', axis=1, tiled=True)  49 us
    all_to_all x1, waiting for transfers between devices, shards(): lax.all_to_all(jnp.stack([extended_two] * lax.axis_size('rows')), 'rows',...  44.8 us
    reshape x6, local copies, waits for them, and re-layouts, causal_conv(): product[:, :folded]  25.9 us
    all_to_all x1, blocking collectives, shards(): lax.all_to_all(conv_two, 'rows', split_axis=1, concat_axis=3, tiled=True)  13.6 us
    all_to_all x1, blocking collectives, shards(): lax.all_to_all(conv_one, 'rows', split_axis=1, concat_axis=3, tiled=True)  12 us
    slice x8, local copies, waits for them, and re-layouts, causal_conv(): slab = padded[tap_time:tap_time + frames]  10.6 us
    dot_general x6, matrix products, causal_conv(): lax.dot_general(slab.reshape(-1, channels), taps, (((1,), (1,)), ((), ())...  8.78 us
    ppermute x2, starting transfers between devices, passed_along(): return lax.ppermute(x, axis, pairs)  7.03 us
  transfers between devices with their start and end apart: 4, of which 4 were waited for; matrix products, arithmetic and copies ran while one was open for 2% of the time, Pallas kernels for 0%

profile of v1, /device:TPU:1, one launch (start us, length us, event | category | flops | bytes accessed | tf_op | source)
XLA Modules:
  0.0 225.4 jit_solution(14026688927869705534)
XLA Ops:
  7.5 0.9 fusion.32
  8.4 3.9 %collective-permute-start = (bf16[2,1,40,384]{3,2,1,0:T(8,128)(2,1)S(1)}, bf16[2,1,40,384]{3,2,1,0:T(8,128)(2,1)S(1)}, u32[]{:S(2)}, u32[]{:S(2)}) collective-permute-start(bf16[2,1,40,384]{3,2,1,0:T(8,128)(2,1)S(1)} %fusion.32), channel_id=1, source_target_pairs={{0,16},{16,32},{32,48},{48,64},{64,80},{80,96},{96,112},{112,128},... | collective-permute-start | bytes 184328 | tf_op jit(solution)/shard_map/ppermute | solution.py:10
  12.4 1.3 collective-permute-done
  15.1 1.1 fusion.35
  16.2 49.0 %all-gather.2.cloned.1.call-done = bf16[4,16,40,384]{3,2,0,1:T(8,128)(2,1)} async-done(((bf16[4,1,40,384]{3,2,0,1:T(8,128)(2,1)}), bf16[4,16,40,384]{3,2,0,1:T(8,128)(2,1)}) %all-gather.2.cloned.1.call-update) | async-done | bytes 1966096 | tf_op jit(solution)/shard_map/all_gather | solution.py:60
  65.2 4.8 %pad_slice_fusion.5 = (bf16[2,18,42,384]{3,2,0,1:T(8,128)(2,1)S(1)}, bf16[2,18,42,384]{3,2,0,1:T(8,128)(2,1)}, bf16[2,18,42,384]{3,2,0,1:T(8,128)(2,1)S(1)}) fusion(bf16[4,16,40,384]{3,2,0,1:T(8,128)(2,1)} %all-gather.2.cloned.1.call-done), kind=kLoop, calls=%fused_computation.5 | loop fusion | bytes 5449728 | tf_op jit(solution)/shard_map/slice | solution.py:31
  70.2 1.3 reshape.163
  71.5 1.9 fusion.38
  73.4 4.3 %reshape.165 = f32[2,18,42,3,3,24]{2,1,0,5,4,3:T(8,128)} reshape(f32[1512,216]{0,1:T(8,128)S(1)} %fusion.38) | data formatting | bytes 2612736 | tf_op jit(solution)/shard_map/reshape | solution.py:40
  77.7 1.5 copy.57
  79.2 1.4 reshape.160
  80.6 1.9 fusion.37
  82.4 4.4 %reshape.162 = f32[2,18,42,3,3,24]{2,1,0,5,4,3:T(8,128)} reshape(f32[1512,216]{0,1:T(8,128)S(1)} %fusion.37) | data formatting | bytes 2612736 | tf_op jit(solution)/shard_map/reshape | solution.py:40
  87.9 4.3 %reshape.159 = f32[2,18,42,3,3,24]{2,1,0,5,4,3:T(8,128)} reshape(f32[1512,216]{0,1:T(8,128)S(1)} %fusion.36) | data formatting | bytes 2612736 | tf_op jit(solution)/shard_map/reshape | solution.py:40
  92.2 7.0 %fusion.14 = bf16[2,16,40,24]{2,1,0,3:T(8,128)(2,1)S(1)} fusion(f32[2,18,42,3,3,24]{2,1,0,5,4,3:T(8,128)} %reshape.165, f32[2,18,42,3,3,24]{2,1,0,5,4,3:T(8,128)} %reshape.162, f32[2,18,42,3,3,24]{2,1,0,5,4,3:T(8,128)} %reshape.159, f32[24]{0:T(128)S(1)} %dynamic_slice.6), kind=kLoop, calls=%fused_computation.47 | loop fusion | flops 860160 | bytes 3379296 | tf_op jit(solution)/shard_map/convert_element_type | solution.py:61
  99.6 12.0 %all_to_all.32 = bf16[16,2,960]{2,1,0:T(2,128)(2,1)S(1)} all-to-all(bf16[16,2,960]{2,1,0:T(2,128)(2,1)S(1)} %reshape.203), channel_id=1, replica_groups=mesh['tm'=32,'rows'=16] {'rows'}, dimensions={0} | all-to-all | bytes 122880 | tf_op jit(solution)/shard_map/all_to_all | solution.py:62
  112.7 3.1 %collective-permute-start.1 = (bf16[2,1,40,384]{3,2,1,0:T(8,128)(2,1)S(1)}, bf16[2,1,40,384]{3,2,1,0:T(8,128)(2,1)S(1)}, u32[]{:S(2)}, u32[]{:S(2)}) collective-permute-start(bf16[2,1,40,384]{3,2,1,0:T(8,128)(2,1)S(1)} %multiply_convert_fusion), channel_id=1, source_target_pairs={{0,16},{16,32},{32,48},{48,64},{64,80},{80,96},{96,112},{112,128},... | collective-permute-start | bytes 184328 | tf_op jit(solution)/shard_map/ppermute | solution.py:10
  115.8 1.3 collective-permute-done.1
  117.1 1.5 stack.2
  118.6 4.7 %all-to-all-start.1 = ((bf16[16,4,1,40,384]{4,3,1,2,0:T(8,128)(2,1)}), bf16[16,4,1,40,384]{4,3,1,2,0:T(8,128)(2,1)S(1)}, u32[]{:S(2)}, u32[]{:S(2)}) async-start(bf16[16,4,1,40,384]{4,3,1,2,0:T(8,128)(2,1)} %stack.2), calls=%async_computation.1 | async-start | bytes 3932160 | tf_op jit(solution)/shard_map/all_to_all | solution.py:67
  124.8 44.8 %all-to-all-done.1 = bf16[16,4,1,40,384]{4,3,1,2,0:T(8,128)(2,1)S(1)} async-done(((bf16[16,4,1,40,384]{4,3,1,2,0:T(8,128)(2,1)}), bf16[16,4,1,40,384]{4,3,1,2,0:T(8,128)(2,1)S(1)}, u32[]{:S(2)}, u32[]{:S(2)}) %all-to-all-start.1) | async-done | bytes 1966112 | tf_op jit(solution)/shard_map/all_to_all | solution.py:67
  169.6 2.3 %pad_slice_fusion.2 = (bf16[2,18,42,384]{3,2,0,1:T(8,128)(2,1)S(1)}, bf16[2,18,42,384]{3,2,0,1:T(8,128)(2,1)}, bf16[2,18,42,384]{3,2,0,1:T(8,128)(2,1)S(1)}) fusion(bf16[4,16,40,384]{3,2,0,1:T(8,128)(2,1)S(1)} %bitcast.211), kind=kLoop, calls=%fused_computation.2 | loop fusion | bytes 5449728 | tf_op jit(solution)/shard_map/slice | solution.py:31
  172.0 1.3 reshape.174
  173.4 1.9 fusion.41
  175.3 4.3 %reshape.176 = f32[2,18,42,3,3,24]{2,1,0,5,4,3:T(8,128)} reshape(f32[1512,216]{0,1:T(8,128)S(1)} %fusion.41) | data formatting | bytes 2612736 | tf_op jit(solution)/shard_map/reshape | solution.py:40
  179.6 1.5 copy.63
  181.1 1.4 reshape.171
  182.4 1.9 fusion.40
  184.3 4.4 %reshape.173 = f32[2,18,42,3,3,24]{2,1,0,5,4,3:T(8,128)} reshape(f32[1512,216]{0,1:T(8,128)S(1)} %fusion.40) | data formatting | bytes 2612736 | tf_op jit(solution)/shard_map/reshape | solution.py:40
  189.8 4.3 %reshape.170 = f32[2,18,42,3,3,24]{2,1,0,5,4,3:T(8,128)} reshape(f32[1512,216]{0,1:T(8,128)S(1)} %fusion.39) | data formatting | bytes 2612736 | tf_op jit(solution)/shard_map/reshape | solution.py:40
  194.1 7.0 %fusion.1 = f32[2,16,40,24]{2,1,0,3:T(8,128)S(1)} fusion(f32[2,18,42,3,3,24]{2,1,0,5,4,3:T(8,128)} %reshape.176, f32[2,18,42,3,3,24]{2,1,0,5,4,3:T(8,128)} %reshape.173, f32[2,18,42,3,3,24]{2,1,0,5,4,3:T(8,128)} %reshape.170, f32[24]{0:T(128)S(1)} %dynamic_slice.7), kind=kLoop, calls=%fused_computation.8 | loop fusion | flops 829440 | bytes 3440736 | tf_op jit(solution)/shard_map/add | solution.py:49
  202.0 13.6 %all_to_all.33 = f32[16,1,1920]{2,1,0:T(1,128)S(1)} all-to-all(f32[16,1,1920]{2,1,0:T(1,128)S(1)} %reshape.205), channel_id=1, replica_groups=mesh['tm'=32,'rows'=16] {'rows'}, dimensions={0} | all-to-all | bytes 245760 | tf_op jit(solution)/shard_map/all_to_all | solution.py:70
  (42 shorter events, 11.6 us)
Async XLA Ops:
  6.5 58.7 %all-gather.2.cloned.1.call-start = ((), (), s32[]{:S(2)}) async-start(), calls=%async_computation.3 | async-start | bytes 2088960 | tf_op jit(solution)/shard_map/all_gather | solution.py:60
  8.4 5.2 %collective-permute-start = (bf16[2,1,40,384]{3,2,1,0:T(8,128)(2,1)S(1)}, bf16[2,1,40,384]{3,2,1,0:T(8,128)(2,1)S(1)}, u32[]{:S(2)}, u32[]{:S(2)}) collective-permute-start(bf16[2,1,40,384]{3,2,1,0:T(8,128)(2,1)S(1)} %fusion.32), channel_id=1, source_target_pairs={{0,16},{16,32},{32,48},{48,64},{64,80},{80,96},{96,112},{112,128},... | collective-permute-start | bytes 184328 | tf_op jit(solution)/shard_map/ppermute | solution.py:10
  99.2 13.4 %copy-start.4 = (f32[384]{0:T(512)S(1)}, f32[384]{0:T(512)}, u32[]{:S(2)}) copy-start(f32[384]{0:T(512)} %param.11) | copy-start | bytes 4612
  112.7 4.4 %collective-permute-start.1 = (bf16[2,1,40,384]{3,2,1,0:T(8,128)(2,1)S(1)}, bf16[2,1,40,384]{3,2,1,0:T(8,128)(2,1)S(1)}, u32[]{:S(2)}, u32[]{:S(2)}) collective-permute-start(bf16[2,1,40,384]{3,2,1,0:T(8,128)(2,1)S(1)} %multiply_convert_fusion), channel_id=1, source_target_pairs={{0,16},{16,32},{32,48},{48,64},{64,80},{80,96},{96,112},{112,128},... | collective-permute-start | bytes 184328 | tf_op jit(solution)/shard_map/ppermute | solution.py:10
  118.6 5.4 %copy-start.3 = (bf16[24,3,3,3,384]{4,0,3,2,1:T(8,128)(2,1)S(1)}, bf16[24,3,3,3,384]{4,0,3,2,1:T(8,128)(2,1)}, u32[]{:S(2)}) copy-start(bf16[24,3,3,3,384]{4,0,3,2,1:T(8,128)(2,1)} %param.12) | copy-start | bytes 1492996
  118.6 51.0 %all-to-all-start.1 = ((bf16[16,4,1,40,384]{4,3,1,2,0:T(8,128)(2,1)}), bf16[16,4,1,40,384]{4,3,1,2,0:T(8,128)(2,1)S(1)}, u32[]{:S(2)}, u32[]{:S(2)}) async-start(bf16[16,4,1,40,384]{4,3,1,2,0:T(8,128)(2,1)} %stack.2), calls=%async_computation.1 | async-start | bytes 3932160 | tf_op jit(solution)/shard_map/all_to_all | solution.py:67
  172.0 1.3 copy-start.1
  181.1 1.4 copy-start
  201.1 16.8 %copy-start.2 = (bf16[2,1,40,384]{3,2,1,0:T(8,128)(2,1)S(1)}, bf16[2,1,40,384]{3,2,1,0:T(8,128)(2,1)}, u32[]{:S(2)}) copy-start(bf16[2,1,40,384]{3,2,1,0:T(8,128)(2,1)} %param.7) | copy-start | bytes 184324
Sparse Core Ops, SparseCore 0:
  14.5 50.7 all-gather.1
